TPU v7x, 32 devices: a whole 2x2x4 slice. The times are simulated.
32 devices in a mesh: ep: 8 (over z, x), tp: 4 (over y, core).
Axes of the slice: x: 2, y: 2, z: 4, core: 2. Of those that a mesh axis runs over, the one named last changes fastest.
Arguments:
- features: bfloat16 [2048, 1024], P('ep'), may hold values from -6 to 6
- cotangent: bfloat16 [2048, 2048], P('ep'), may hold values from -6 to 6
- expert_ids: int32 [2048, 2], P('ep'), may hold values from 0 to 7, all different within a row; in each aligned block of 256 rows (0 to 255, 256 to 511, ...) at most 96 rows name the same one
- gate_levels: int32 [2048, 2], P('ep'), may hold values from 1 to 15
- w_in: bfloat16 [8, 1024, 4096], P('ep', None, 'tp'), may hold values from -0.1875 to 0.1875
- w_out: bfloat16 [8, 4096, 2048], P('ep', 'tp'), may hold values from -0.09375 to 0.09375
Outputs:
- grad_in: bfloat16 [2048, 1024], P('ep', 'tp')
- grad_w_in: bfloat16 [8, 1024, 4096], P('ep', None, 'tp')
- grad_w_out: bfloat16 [8, 4096, 2048], P('ep', 'tp')
Inputs may be any that keep to these rules, and one draw needn't show every extreme that they name: `expert_ids`: each row names two different experts. In each aligned block of 256 rows no expert is named by more than 96 rows, and some expert reaches 96 rows in some block.
All inputs are finite; a program needn't handle non-finite values.
Results may differ from a plain program's by a relative error of at most 0.0065.
Values may be sent and summed in bfloat16 or wider, within the bound.
No kernel may reach another device: no remote copies, remote signals or barrier semaphores. Data moves between devices by JAX's collectives and lax.ppermute only.
A program may use at most 128 MiB of HBM per device.

v0:
```python
import math
import jax
import jax.numpy as jnp
from jax import lax
from jax.sharding import PartitionSpec as P

E = 8


def shifted(value, axis, by):
    peers = lax.axis_size(axis)
    return lax.ppermute(value, axis, [(i, (i + by) % peers) for i in range(peers)])


def slot_positions(expert_ids, blocks, experts, capacity):
    flattened = expert_ids.reshape(blocks, -1)
    one_hot = (flattened[:, :, None] == jnp.arange(experts, dtype=jnp.int32)[None, None, :]).astype(
        jnp.int32
    )
    earlier = jnp.cumsum(one_hot, axis=1) - one_hot
    within = jnp.sum(one_hot * earlier, axis=2)
    block_ids = jnp.arange(blocks, dtype=jnp.int32)[:, None]
    return ((block_ids * experts + flattened) * capacity + within).reshape(-1)


def chip_then_link_sum(partial, j):
    quarter = partial.shape[0] // 4

    def rows(q):
        return lax.dynamic_slice_in_dim(partial, q * quarter, quarter, 0)

    keep = jnp.concatenate([rows(j), rows(j ^ 2)], axis=0)
    give = jnp.concatenate([rows(j ^ 1), rows(j ^ 3)], axis=0)
    keep = keep + lax.ppermute(give, "tp", [(i, i ^ 1) for i in range(4)])
    mine, send = (keep[:quarter], keep[quarter:])
    moved = lax.ppermute(send.astype(jnp.bfloat16), "tp", [(i, i ^ 2) for i in range(4)])
    return mine + moved.astype(jnp.float32)


def shards(features, cotangent, expert_ids, gate_levels, w_in, w_out):
    device_count = lax.axis_size("ep")
    replicas = device_count // E
    replica = lax.axis_index("ep") // E
    tokens_here = expert_ids.shape[0]
    sub_rows = tokens_here // replicas
    capacity = 3 * sub_rows // 8
    slot_count = device_count * capacity
    pair_count = 2 * tokens_here
    positions = slot_positions(expert_ids, replicas, E, capacity)
    slot_ids = jnp.arange(slot_count, dtype=jnp.int32)[:, None]
    choices = positions.reshape(tokens_here, 2)
    first_hit = choices[None, :, 0] == slot_ids
    second_hit = choices[None, :, 1] == slot_ids
    gates = gate_levels.astype(jnp.float32) / 16.0
    pick = (first_hit | second_hit).astype(jnp.bfloat16)
    pick_scaled = jnp.where(
        first_hit, gates[None, :, 0], jnp.where(second_hit, gates[None, :, 1], 0.0)
    ).astype(jnp.bfloat16)
    tp_size = lax.axis_size("tp")
    tp_index = lax.axis_index("tp")
    split = 4 if tp_size == 4 else 2 if tp_size % 2 == 0 else 1

    def dispatched(table, selection):
        width = table.shape[1] // split
        part = tp_index % split
        mine = lax.dynamic_slice_in_dim(table, part * width, width, 1)
        mine = jnp.dot(selection, mine, preferred_element_type=jnp.float32).astype(jnp.bfloat16)
        mine = lax.all_to_all(mine, "ep", split_axis=0, concat_axis=0, tiled=True)
        pieces = [(mine, part)]
        if split == 4:
            across = lax.ppermute(mine, "tp", [(i, i ^ 2) for i in range(tp_size)])
            pieces.append((across, part ^ 2))
        if split >= 2:
            pieces += [
                (lax.ppermute(piece, "tp", [(i, i ^ 1) for i in range(tp_size)]), where ^ 1)
                for piece, where in pieces
            ]
        if split == 1:
            return mine
        whole = jnp.zeros((mine.shape[0], table.shape[1]), jnp.bfloat16)
        for piece, where in pieces:
            whole = lax.dynamic_update_slice_in_dim(whole, piece, where * width, 1)
        return whole

    rows_x = dispatched(features, pick)
    rows_dy = dispatched(cotangent, pick_scaled)
    piece_in = w_in[0]
    piece_out = w_out[0]
    span = piece_in.shape[1]
    weight_in = jnp.zeros((piece_in.shape[0], span * replicas), jnp.bfloat16)
    weight_out = jnp.zeros((span * replicas, piece_out.shape[1]), jnp.bfloat16)
    weight_in = lax.dynamic_update_slice_in_dim(weight_in, piece_in, replica * span, 1)
    weight_out = lax.dynamic_update_slice_in_dim(weight_out, piece_out, replica * span, 0)
    moving = (piece_in, piece_out)
    for turn_index in range(1, replicas):
        moving = shifted((moving[0], moving[1]), "ep", E)
        anchor = (replica - turn_index) % replicas
        weight_in = lax.dynamic_update_slice_in_dim(weight_in, moving[0], anchor * span, 1)
        weight_out = lax.dynamic_update_slice_in_dim(weight_out, moving[1], anchor * span, 0)
    pre = jnp.dot(rows_x, weight_in, preferred_element_type=jnp.float32)
    activated, gelu_back = jax.vjp(jax.nn.gelu, pre)
    act_rows = lax.optimization_barrier(activated.astype(jnp.bfloat16))
    back_act = lax.dot_general(
        rows_dy, weight_out, (((1,), (1,)), ((), ())), preferred_element_type=jnp.float32
    )
    back_pre = gelu_back(back_act)[0].astype(jnp.bfloat16)
    partial = lax.dot_general(
        weight_in, back_pre, (((1,), (1,)), ((), ())), preferred_element_type=jnp.float32
    )
    if tp_size == 4:
        summed = chip_then_link_sum(partial, tp_index)
    else:
        summed = lax.psum_scatter(partial, "tp", scatter_dimension=0, tiled=True)
    returned = lax.all_to_all(
        summed.astype(jnp.bfloat16), "ep", split_axis=1, concat_axis=1, tiled=True
    )
    grad_in = lax.dot_general(
        pick, returned, (((0,), (1,)), ((), ())), preferred_element_type=jnp.float32
    ).astype(jnp.bfloat16)

    def span_grads(first_span, span_total):
        width = span_total * span
        act_cols = lax.dynamic_slice_in_dim(act_rows, first_span * span, width, 1)
        pre_cols = lax.dynamic_slice_in_dim(back_pre, first_span * span, width, 1)
        grad_first = lax.dot_general(
            pre_cols, rows_x, (((0,), (0,)), ((), ())), preferred_element_type=jnp.float32
        )
        grad_second = lax.dot_general(
            act_cols, rows_dy, (((0,), (0,)), ((), ())), preferred_element_type=jnp.float32
        )
        return (grad_first, grad_second)

    summed_grads = span_grads((replica - 1) % replicas, 1)
    for turn_index in range(1, replicas):
        summed_grads = shifted((summed_grads[0], summed_grads[1]), "ep", E)
        own_grads = span_grads((replica - turn_index - 1) % replicas, 1)
        summed_grads = (summed_grads[0] + own_grads[0], summed_grads[1] + own_grads[1])
    grad_scale = 1.0 / math.sqrt(2.0 * tokens_here * device_count / E)
    grad_w_in = (summed_grads[0] * grad_scale).T.astype(jnp.bfloat16)[None]
    grad_w_out = (summed_grads[1] * grad_scale).astype(jnp.bfloat16)[None]
    return (grad_in, grad_w_in, grad_w_out)


def solution(mesh):
    return jax.shard_map(
        shards,
        mesh=mesh,
        in_specs=(
            P("ep", None),
            P("ep", None),
            P("ep", None),
            P("ep", None),
            P("ep", None, "tp"),
            P("ep", "tp", None),
        ),
        out_specs=(P("ep", "tp"), P("ep", None, "tp"), P("ep", "tp", None)),
        check_vma=False,
    )
```

profile of v0, /device:TPU:0, one launch (start us, length us, event | category | flops | bytes accessed | tf_op | source)
XLA Modules:
  0.0 114.2 jit_solution(2538549996480562133)
XLA Ops:
  1.8 1.1 %reduce-window.6 = s32[1,8,4,128]{3,1,2,0:T(8,128)S(1)} reduce-window(s32[1,8,4,128]{3,1,2,0:T(8,128)S(1)} %convert_bitcast_fusion, s32[]{:T(128)} %constant.31.clone.1), window={size=1x1x1x128 pad=0_0x0_0x0_0x127_0}, to_apply=%region_0.1 | reduce-window | flops 520192 | bytes 32772 | tf_op jit(solution)/shard_map/reduce-window
  4.2 1.9 %convolution_convert_fusion.1 = bf16[768,256]{1,0:T(8,128)(2,1)} fusion(s32[256]{0:T(256)S(1)} %bitcast.69, s32[256]{0:T(256)S(1)} %bitcast.66, bf16[256,1024]{1,0:T(8,128)(2,1)} %param.6, s32[]{:T(128)S(6)} %select_n.70), kind=kOutput, calls=%fused_computation.23 | convolution fusion | flops 101449728 | bytes 526340 | tf_op jit(solution)/shard_map/dot_general | solution.py:67
  6.2 7.3 %all-to-all-start.1 = ((bf16[8,96,256]{2,1,0:T(8,128)(2,1)}), bf16[8,96,256]{2,1,0:T(8,128)(2,1)S(1)}, u32[]{:S(2)}, u32[]{:S(2)}) async-start(bf16[8,96,256]{2,1,0:T(8,128)(2,1)} %bitcast.13), calls=%async_computation.1 | async-start | bytes 786432 | tf_op jit(solution)/shard_map/all_to_all | solution.py:68
  14.1 2.2 %convolution_convert_fusion = bf16[768,512]{1,0:T(8,128)(2,1)} fusion(f32[256]{0:T(256)S(1)} %bitcast.73, f32[256]{0:T(256)S(1)} %bitcast.72, s32[256]{0:T(256)S(1)} %bitcast.70, s32[256]{0:T(256)S(1)} %bitcast.67, bf16[256,2048]{1,0:T(8,128)(2,1)} %param.7, s32[]{:T(128)S(6)} %select_n.66), kind=kOutput, calls=%fused_computation.22 | convolution fusion | flops 202506240 | bytes 1052676 | tf_op jit(solution)/shard_map/dot_general | solution.py:67
  16.3 8.8 %all-to-all-done.1 = bf16[8,96,256]{2,1,0:T(8,128)(2,1)S(1)} async-done(((bf16[8,96,256]{2,1,0:T(8,128)(2,1)}), bf16[8,96,256]{2,1,0:T(8,128)(2,1)S(1)}, u32[]{:S(2)}, u32[]{:S(2)}) %all-to-all-start.1) | async-done | bytes 393248 | tf_op jit(solution)/shard_map/all_to_all | solution.py:68
  25.1 3.6 %all-to-all-start = ((bf16[8,96,512]{2,1,0:T(8,128)(2,1)}), bf16[8,96,512]{2,1,0:T(8,128)(2,1)S(1)}, u32[]{:S(2)}, u32[]{:S(2)}) async-start(bf16[8,96,512]{2,1,0:T(8,128)(2,1)} %bitcast.63), calls=%async_computation | async-start | bytes 1572864 | tf_op jit(solution)/shard_map/all_to_all | solution.py:68
  28.8 1.5 %collective-permute-start.3 = (bf16[768,256]{1,0:T(8,128)(2,1)S(1)}, bf16[768,256]{1,0:T(8,128)(2,1)}, u32[]{:S(2)}, u32[]{:S(2)}) collective-permute-start(bf16[768,256]{1,0:T(8,128)(2,1)S(1)} %bitcast.60), channel_id=1, source_target_pairs={{0,2},{1,3},{2,0},{3,1},{4,6},{5,7},{6,4},{7,5},{8,10},{9,11},{10,... | collective-permute-start | bytes 1179656 | tf_op jit(solution)/shard_map/ppermute | solution.py:71
  30.3 18.6 %all-to-all-done = bf16[8,96,512]{2,1,0:T(8,128)(2,1)S(1)} async-done(((bf16[8,96,512]{2,1,0:T(8,128)(2,1)}), bf16[8,96,512]{2,1,0:T(8,128)(2,1)S(1)}, u32[]{:S(2)}, u32[]{:S(2)}) %all-to-all-start) | async-done | bytes 786464 | tf_op jit(solution)/shard_map/all_to_all | solution.py:68
  48.9 1.5 %collective-permute-start = (bf16[768,512]{1,0:T(8,128)(2,1)S(1)}, bf16[768,512]{1,0:T(8,128)(2,1)}, u32[]{:S(2)}, u32[]{:S(2)}) collective-permute-start(bf16[768,512]{1,0:T(8,128)(2,1)S(1)} %bitcast.57), channel_id=1, source_target_pairs={{0,2},{1,3},{2,0},{3,1},{4,6},{5,7},{6,4},{7,5},{8,10},{9,11},{10,... | collective-permute-start | bytes 2359304 | tf_op jit(solution)/shard_map/ppermute | solution.py:71
  51.2 1.0 constant_dynamic-update-slice_fusion.2
  52.3 1.0 constant_dynamic-update-slice_fusion.1
  54.1 12.8 %collective-permute-done = bf16[768,512]{1,0:T(8,128)(2,1)} collective-permute-done((bf16[768,512]{1,0:T(8,128)(2,1)S(1)}, bf16[768,512]{1,0:T(8,128)(2,1)}, u32[]{:S(2)}, u32[]{:S(2)}) %collective-permute-start) | collective-permute-done | bytes 786464 | tf_op jit(solution)/shard_map/ppermute | solution.py:71
  66.9 3.5 %multiply_convert_fusion.2 = (bf16[768,1024]{1,0:T(8,128)(2,1)}, f32[768,1024]{1,0:T(8,128)S(1)}) fusion(bf16[768,1024]{1,0:T(8,128)(2,1)S(1)} %constant_dynamic-update-slice_fusion, bf16[1,1024,1024]{2,1,0:T(8,128)(2,1)S(1)} %copy-done), kind=kOutput, calls=%fused_computation.14 | convolution fusion | flops 1617690624 | bytes 8388608 | tf_op jit(solution)/shard_map/dot_general | solution.py:100
  70.4 1.4 %constant_dynamic-update-slice_fusion.6 = bf16[768,2048]{1,0:T(8,128)(2,1)S(1)} fusion(bf16[768,2048]{1,0:T(8,128)(2,1)S(1)} %constant_dynamic-update-slice_fusion.7, bf16[768,512]{1,0:T(8,128)(2,1)} %collective-permute-done, s32[]{:T(128)S(6)} %select_n.67), kind=kLoop, calls=%fused_computation.61 | loop fusion | bytes 1572868 | tf_op jit(solution)/shard_map/dynamic_update_slice | solution.py:82
  72.8 5.0 %fusion.9 = bf16[768,1024]{1,0:T(8,128)(2,1)S(1)} fusion(f32[768,1024]{1,0:T(8,128)S(1)} %get-tuple-element.12, bf16[768,2048]{1,0:T(8,128)(2,1)S(1)} %constant_dynamic-update-slice_fusion.4, bf16[1,1024,2048]{2,1,0:T(8,128)(2,1)S(1)} %copy-done.2), kind=kOutput, calls=%fused_computation.13 | convolution fusion | flops 3236954112 | bytes 12058624 | tf_op jit(solution)/shard_map/dot_general | solution.py:103
  77.8 1.8 %fusion.12 = f32[768,1024]{1,0:T(8,128)S(1)} fusion(bf16[768,1024]{1,0:T(8,128)(2,1)S(1)} %fusion.9, bf16[1,1024,1024]{2,1,0:T(8,128)(2,1)S(1)} %copy-done), kind=kOutput, calls=%fused_computation.15 | convolution fusion | flops 1610612736 | bytes 6815744 | tf_op jit(solution)/shard_map/dot_general | solution.py:107
  80.9 3.0 %collective-permute-done.6 = f32[512,768]{0,1:T(8,128)S(1)} collective-permute-done((f32[512,768]{0,1:T(8,128)S(1)}, f32[512,768]{0,1:T(8,128)S(1)}, u32[]{:S(2)}, u32[]{:S(2)}) %collective-permute-start.6) | collective-permute-done | bytes 1572896 | tf_op jit(solution)/shard_map/ppermute | solution.py:34
  84.2 1.6 %collective-permute-start.7 = (bf16[256,768]{0,1:T(8,128)(2,1)S(1)}, bf16[256,768]{0,1:T(8,128)(2,1)S(1)}, u32[]{:S(2)}, u32[]{:S(2)}) collective-permute-start(bf16[256,768]{0,1:T(8,128)(2,1)S(1)} %slice.46), channel_id=1, source_target_pairs={{0,2},{1,3},{2,0},{3,1},{4,6},{5,7},{6,4},{7,5},{8,10},{9,11},{10,... | collective-permute-start | bytes 1179656 | tf_op jit(solution)/shard_map/ppermute | solution.py:36
  85.8 3.2 %fusion.16 = bf16[1,1024,1024]{2,1,0:T(8,128)(2,1)} fusion(bf16[768,1024]{1,0:T(8,128)(2,1)S(1)} %constant_dynamic-update-slice_fusion, bf16[768,1024]{1,0:T(8,128)(2,1)S(1)} %fusion.9), kind=kOutput, calls=%fused_computation.19 | convolution fusion | flops 1612709888 | bytes 5242880 | tf_op jit(solution)/shard_map/dot_general | solution.py:125
  89.0 6.7 %collective-permute-done.7 = bf16[256,768]{0,1:T(8,128)(2,1)S(1)} collective-permute-done((bf16[256,768]{0,1:T(8,128)(2,1)S(1)}, bf16[256,768]{0,1:T(8,128)(2,1)S(1)}, u32[]{:S(2)}, u32[]{:S(2)}) %collective-permute-start.7) | collective-permute-done | bytes 393248 | tf_op jit(solution)/shard_map/ppermute | solution.py:36
  96.6 5.1 %all-to-all-start.2 = ((bf16[256,8,96]{0,2,1:T(8,128)(2,1)}), bf16[256,8,96]{0,2,1:T(8,128)(2,1)S(1)}, u32[]{:S(2)}, u32[]{:S(2)}) async-start(bf16[256,8,96]{0,2,1:T(8,128)(2,1)} %bitcast.20), calls=%async_computation.2 | async-start | bytes 786432 | tf_op jit(solution)/shard_map/all_to_all | solution.py:114
  101.7 7.9 %fusion.2 = bf16[1,1024,2048]{2,1,0:T(8,128)(2,1)} fusion(bf16[768,1024]{1,0:T(8,128)(2,1)} %get-tuple-element.11, bf16[768,2048]{1,0:T(8,128)(2,1)} %copy-done.1), kind=kOutput, calls=%fused_computation.6 | convolution fusion | flops 3225419776 | bytes 8912896 | tf_op jit(solution)/shard_map/dot_general | solution.py:128
  109.6 3.5 %all-to-all-done.2 = bf16[256,8,96]{0,2,1:T(8,128)(2,1)S(1)} async-done(((bf16[256,8,96]{0,2,1:T(8,128)(2,1)}), bf16[256,8,96]{0,2,1:T(8,128)(2,1)S(1)}, u32[]{:S(2)}, u32[]{:S(2)}) %all-to-all-start.2) | async-done | bytes 393248 | tf_op jit(solution)/shard_map/all_to_all | solution.py:114
  113.1 1.1 convolution_convert_fusion.2
  (41 shorter events, 8.0 us)
Async XLA Ops:
  0.6 66.2 %copy-start = (bf16[1,1024,1024]{2,1,0:T(8,128)(2,1)S(1)}, bf16[1,1024,1024]{2,1,0:T(8,128)(2,1)}, u32[]{:S(2)}) copy-start(bf16[1,1024,1024]{2,1,0:T(8,128)(2,1)} %param.10) | copy-start | bytes 6291460
  6.2 19.0 %all-to-all-start.1 = ((bf16[8,96,256]{2,1,0:T(8,128)(2,1)}), bf16[8,96,256]{2,1,0:T(8,128)(2,1)S(1)}, u32[]{:S(2)}, u32[]{:S(2)}) async-start(bf16[8,96,256]{2,1,0:T(8,128)(2,1)} %bitcast.13), calls=%async_computation.1 | async-start | bytes 786432 | tf_op jit(solution)/shard_map/all_to_all | solution.py:68
  25.1 23.8 %all-to-all-start = ((bf16[8,96,512]{2,1,0:T(8,128)(2,1)}), bf16[8,96,512]{2,1,0:T(8,128)(2,1)S(1)}, u32[]{:S(2)}, u32[]{:S(2)}) async-start(bf16[8,96,512]{2,1,0:T(8,128)(2,1)} %bitcast.63), calls=%async_computation | async-start | bytes 1572864 | tf_op jit(solution)/shard_map/all_to_all | solution.py:68
  28.8 21.7 %collective-permute-start.3 = (bf16[768,256]{1,0:T(8,128)(2,1)S(1)}, bf16[768,256]{1,0:T(8,128)(2,1)}, u32[]{:S(2)}, u32[]{:S(2)}) collective-permute-start(bf16[768,256]{1,0:T(8,128)(2,1)S(1)} %bitcast.60), channel_id=1, source_target_pairs={{0,2},{1,3},{2,0},{3,1},{4,6},{5,7},{6,4},{7,5},{8,10},{9,11},{10,... | collective-permute-start | bytes 1179656 | tf_op jit(solution)/shard_map/ppermute | solution.py:71
  48.9 18.0 %collective-permute-start = (bf16[768,512]{1,0:T(8,128)(2,1)S(1)}, bf16[768,512]{1,0:T(8,128)(2,1)}, u32[]{:S(2)}, u32[]{:S(2)}) collective-permute-start(bf16[768,512]{1,0:T(8,128)(2,1)S(1)} %bitcast.57), channel_id=1, source_target_pairs={{0,2},{1,3},{2,0},{3,1},{4,6},{5,7},{6,4},{7,5},{8,10},{9,11},{10,... | collective-permute-start | bytes 2359304 | tf_op jit(solution)/shard_map/ppermute | solution.py:71
  50.4 1.9 %collective-permute-start.4 = (bf16[768,256]{1,0:T(8,128)(2,1)S(1)}, bf16[768,256]{1,0:T(8,128)(2,1)}, u32[]{:S(2)}, u32[]{:S(2)}) collective-permute-start(bf16[768,256]{1,0:T(8,128)(2,1)S(1)} %bitcast.61), channel_id=1, source_target_pairs={{0,1},{1,0},{2,3},{3,2},{4,5},{5,4},{6,7},{7,6},{8,9},{9,8},{10,11... | collective-permute-start | bytes 1179656 | tf_op jit(solution)/shard_map/ppermute | solution.py:75
  50.4 3.6 %collective-permute-start.5 = (bf16[768,256]{1,0:T(8,128)(2,1)}, bf16[768,256]{1,0:T(8,128)(2,1)S(1)}, u32[]{:S(2)}, u32[]{:S(2)}) collective-permute-start(bf16[768,256]{1,0:T(8,128)(2,1)} %collective-permute-done.3), channel_id=1, source_target_pairs={{0,1},{1,0},{2,3},{3,2},{4,5},{5,4},{6,7},{7,6},{8,9},{9,8},{10,11... | collective-permute-start | bytes 1179656 | tf_op jit(solution)/shard_map/ppermute | solution.py:75
  53.3 18.5 %collective-permute-start.1 = (bf16[768,512]{1,0:T(8,128)(2,1)S(1)}, bf16[768,512]{1,0:T(8,128)(2,1)S(1)}, u32[]{:S(2)}, u32[]{:S(2)}) collective-permute-start(bf16[768,512]{1,0:T(8,128)(2,1)S(1)} %bitcast.58), channel_id=1, source_target_pairs={{0,1},{1,0},{2,3},{3,2},{4,5},{5,4},{6,7},{7,6},{8,9},{9,8},{10,11... | collective-permute-start | bytes 2359304 | tf_op jit(solution)/shard_map/ppermute | solution.py:75
  66.9 5.0 %collective-permute-start.2 = (bf16[768,512]{1,0:T(8,128)(2,1)}, bf16[768,512]{1,0:T(8,128)(2,1)S(1)}, u32[]{:S(2)}, u32[]{:S(2)}) collective-permute-start(bf16[768,512]{1,0:T(8,128)(2,1)} %collective-permute-done), channel_id=1, source_target_pairs={{0,1},{1,0},{2,3},{3,2},{4,5},{5,4},{6,7},{7,6},{8,9},{9,8},{10,11... | collective-permute-start | bytes 2359304 | tf_op jit(solution)/shard_map/ppermute | solution.py:75
  70.4 2.4 %copy-start.2 = (bf16[1,1024,2048]{2,1,0:T(8,128)(2,1)S(1)}, bf16[1,1024,2048]{2,1,0:T(8,128)(2,1)}, u32[]{:S(2)}) copy-start(bf16[1,1024,2048]{2,1,0:T(8,128)(2,1)} %param.11) | copy-start | bytes 12582916
  72.0 5.8 %copy-start.1 = (bf16[768,2048]{1,0:T(8,128)(2,1)}, bf16[768,2048]{1,0:T(8,128)(2,1)S(1)}, u32[]{:S(2)}) copy-start(bf16[768,2048]{1,0:T(8,128)(2,1)S(1)} %constant_dynamic-update-slice_fusion.4) | copy-start | bytes 9437188
  80.3 3.6 %collective-permute-start.6 = (f32[512,768]{0,1:T(8,128)S(1)}, f32[512,768]{0,1:T(8,128)S(1)}, u32[]{:S(2)}, u32[]{:S(2)}) collective-permute-start(f32[512,768]{0,1:T(8,128)S(1)} %pad_maximum_fusion), channel_id=1, source_target_pairs={{0,1},{1,0},{2,3},{3,2},{4,5},{5,4},{6,7},{7,6},{8,9},{9,8},{10,11... | collective-permute-start | bytes 4718600 | tf_op jit(solution)/shard_map/ppermute | solution.py:34
  84.2 11.5 %collective-permute-start.7 = (bf16[256,768]{0,1:T(8,128)(2,1)S(1)}, bf16[256,768]{0,1:T(8,128)(2,1)S(1)}, u32[]{:S(2)}, u32[]{:S(2)}) collective-permute-start(bf16[256,768]{0,1:T(8,128)(2,1)S(1)} %slice.46), channel_id=1, source_target_pairs={{0,2},{1,3},{2,0},{3,1},{4,6},{5,7},{6,4},{7,5},{8,10},{9,11},{10,... | collective-permute-start | bytes 1179656 | tf_op jit(solution)/shard_map/ppermute | solution.py:36
  96.6 16.5 %all-to-all-start.2 = ((bf16[256,8,96]{0,2,1:T(8,128)(2,1)}), bf16[256,8,96]{0,2,1:T(8,128)(2,1)S(1)}, u32[]{:S(2)}, u32[]{:S(2)}) async-start(bf16[256,8,96]{0,2,1:T(8,128)(2,1)} %bitcast.20), calls=%async_computation.2 | async-start | bytes 786432 | tf_op jit(solution)/shard_map/all_to_all | solution.py:114
where the time goes:
time: 115 us; the launch traced here: 114 us
  waiting for transfers between devices  53.5 us (47%)
  matrix products  26.6 us (23%)
  starting transfers between devices  22 us (19%)
  local copies, waits for them, and re-layouts  7.22 us (6%)
  other arithmetic  4.03 us (4%)
    all_to_all x2, waiting for transfers between devices, dispatched(): mine = lax.all_to_all(mine, 'ep', split_axis=0, concat_axis=0, tiled=True)  27.4 us
    ppermute x2, waiting for transfers between devices, dispatched(): across = lax.ppermute(mine, 'tp', [(i, i ^ 2) for i in range(tp_size)])  12.8 us
    all_to_all x2, starting transfers between devices, dispatched(): mine = lax.all_to_all(mine, 'ep', split_axis=0, concat_axis=0, tiled=True)  10.9 us
    dot_general x1, matrix products, span_grads(): lax.dot_general(act_cols, rows_dy, (((0,), (0,)), ((), ())), preferred_el...  7.86 us
    ppermute x1, waiting for transfers between devices, chip_then_link_sum(): lax.ppermute(send.astype(jnp.bfloat16), 'tp', [(i, i ^ 2) for i in range(...  6.71 us
    all_to_all x1, starting transfers between devices, shards(): lax.all_to_all(summed.astype(jnp.bfloat16), 'ep', split_axis=1, concat_ax...  5.11 us
    dot_general x1, matrix products, shards(): lax.dot_general(rows_dy, weight_out, (((1,), (1,)), ((), ())), preferred_...  5.04 us
    dot_general x2, matrix products, dispatched(): jnp.dot(selection, mine, preferred_element_type=jnp.float32)  4.14 us
  transfers between devices with their start and end apart: 11, of which 6 were waited for; matrix products, arithmetic and copies ran while one was open for 19% of the time, Pallas kernels for 0%

commit v1 on v0

--- a/solution.py
+++ b/solution.py
@@ -5,6 +5,22 @@
 from jax.sharding import PartitionSpec as P
 
 E = 8
+
+
+def pairwise_exchange(x, axis, split, join):
+    ways, here = (lax.axis_size(axis), lax.axis_index(axis))
+    width = x.shape[split] // ways
+    lengths = list(x.shape)
+    lengths[split] = width
+    height = lengths[join]
+    lengths[join] = height * ways
+    full = jnp.zeros(lengths, x.dtype)
+    for mask in range(ways):
+        part = lax.dynamic_slice_in_dim(x, (here ^ mask) * width, width, axis=split)
+        if mask:
+            part = lax.ppermute(part, axis, [(d, d ^ mask) for d in range(ways)])
+        full = lax.dynamic_update_slice_in_dim(full, part, (here ^ mask) * height, axis=join)
+    return full
 
 
 def shifted(value, axis, by):
@@ -111,9 +127,7 @@
         summed = chip_then_link_sum(partial, tp_index)
     else:
         summed = lax.psum_scatter(partial, "tp", scatter_dimension=0, tiled=True)
-    returned = lax.all_to_all(
-        summed.astype(jnp.bfloat16), "ep", split_axis=1, concat_axis=1, tiled=True
-    )
+    returned = pairwise_exchange(summed.astype(jnp.bfloat16), "ep", 1, 1)
     grad_in = lax.dot_general(
         pick, returned, (((0,), (1,)), ((), ())), preferred_element_type=jnp.float32
     ).astype(jnp.bfloat16)

time: 115 us -> 124 us (1.078)
  starting transfers between devices: 22 us -> 26.5 us
  waiting for transfers between devices: 53.5 us -> 57.5 us
  matrix products: 26.6 us -> 23.8 us
  other arithmetic: 4.03 us -> 6.16 us
    ppermute x0 -> x7, starting transfers between devices: none -> 9.77 us  [pairwise_exchange(): part = lax.ppermute(part, axis, [(d, d ^ mask) for d in range(ways)])]
    ppermute x0 -> x7, waiting for transfers between devices: none -> 9.06 us  [pairwise_exchange(): part = lax.ppermute(part, axis, [(d, d ^ mask) for d in range(ways)])]
    all_to_all x1 -> x0, starting transfers between devices: 5.11 us -> none  [shards(): lax.all_to_all(summed.astype(jnp.bfloat16), 'ep', split_axis=1, concat_ax...]
    all_to_all x1 -> x0, waiting for transfers between devices: 3.54 us -> none  [shards(): lax.all_to_all(summed.astype(jnp.bfloat16), 'ep', split_axis=1, concat_ax...]
    dot_general x1, matrix products: 7.86 us -> 5.05 us  [span_grads(): lax.dot_general(act_cols, rows_dy, (((0,), (0,)), ((), ())), preferred_el...]
    ppermute x1, waiting for transfers between devices: 6.71 us -> 4.83 us  [chip_then_link_sum(): lax.ppermute(send.astype(jnp.bfloat16), 'tp', [(i, i ^ 2) for i in range(...]
    add x1, other arithmetic: 0.26 us -> 1.93 us  [chip_then_link_sum(): keep = keep + lax.ppermute(give, 'tp', [(i, i ^ 1) for i in range(4)])]
  transfers between devices with their start and end apart: 11 -> 17, of which waited for: 6 -> 7; matrix products, arithmetic and copies ran while one was open for 19% -> 15% of each run, Pallas kernels for 0% -> 0%
where the time goes in v1:
time: 124 us; the launch traced here: 123 us
  waiting for transfers between devices  57.5 us (46%)
  starting transfers between devices  26.5 us (21%)
  matrix products  23.8 us (19%)
  local copies, waits for them, and re-layouts  8.29 us (7%)
  other arithmetic  6.16 us (5%)
    all_to_all x2, waiting for transfers between devices, dispatched(): mine = lax.all_to_all(mine, 'ep', split_axis=0, concat_axis=0, tiled=True)  27.4 us
    ppermute x2, waiting for transfers between devices, dispatched(): across = lax.ppermute(mine, 'tp', [(i, i ^ 2) for i in range(tp_size)])  12.8 us
    all_to_all x2, starting transfers between devices, dispatched(): mine = lax.all_to_all(mine, 'ep', split_axis=0, concat_axis=0, tiled=True)  10.9 us
    ppermute x7, starting transfers between devices, pairwise_exchange(): part = lax.ppermute(part, axis, [(d, d ^ mask) for d in range(ways)])  9.77 us
    ppermute x7, waiting for transfers between devices, pairwise_exchange(): part = lax.ppermute(part, axis, [(d, d ^ mask) for d in range(ways)])  9.06 us
    dot_general x1, matrix products, span_grads(): lax.dot_general(act_cols, rows_dy, (((0,), (0,)), ((), ())), preferred_el...  5.05 us
    dot_general x1, matrix products, shards(): lax.dot_general(rows_dy, weight_out, (((1,), (1,)), ((), ())), preferred_...  5.05 us
    ppermute x1, waiting for transfers between devices, chip_then_link_sum(): lax.ppermute(send.astype(jnp.bfloat16), 'tp', [(i, i ^ 2) for i in range(...  4.83 us
  transfers between devices with their start and end apart: 17, of which 7 were waited for; matrix products, arithmetic and copies ran while one was open for 15% of the time, Pallas kernels for 0%

profile of v1, /device:TPU:0, one launch (start us, length us, event | category | flops | bytes accessed | tf_op | source)
XLA Modules:
  0.0 123.2 jit_solution(383504248467697663)
XLA Ops:
  4.2 1.9 %convolution_convert_fusion.1 = bf16[768,256]{1,0:T(8,128)(2,1)} fusion(s32[256]{0:T(256)S(1)} %bitcast.66, s32[256]{0:T(256)S(1)} %bitcast.63, bf16[256,1024]{1,0:T(8,128)(2,1)} %param.6, s32[]{:T(128)S(6)} %select_n.102), kind=kOutput, calls=%fused_computation.23 | convolution fusion | flops 101449728 | bytes 526340 | tf_op jit(solution)/shard_map/dot_general | solution.py:83
  6.2 7.3 %all-to-all-start.1 = ((bf16[8,96,256]{2,1,0:T(8,128)(2,1)}), bf16[8,96,256]{2,1,0:T(8,128)(2,1)S(1)}, u32[]{:S(2)}, u32[]{:S(2)}) async-start(bf16[8,96,256]{2,1,0:T(8,128)(2,1)} %bitcast.13), calls=%async_computation.1 | async-start | bytes 786432 | tf_op jit(solution)/shard_map/all_to_all | solution.py:84
  14.1 2.2 %convolution_convert_fusion = bf16[768,512]{1,0:T(8,128)(2,1)} fusion(f32[256]{0:T(256)S(1)} %bitcast.70, f32[256]{0:T(256)S(1)} %bitcast.69, s32[256]{0:T(256)S(1)} %bitcast.67, s32[256]{0:T(256)S(1)} %bitcast.64, bf16[256,2048]{1,0:T(8,128)(2,1)} %param.7, s32[]{:T(128)S(6)} %select_n.98), kind=kOutput, calls=%fused_computation.22 | convolution fusion | flops 202506240 | bytes 1052676 | tf_op jit(solution)/shard_map/dot_general | solution.py:83
  16.3 8.8 %all-to-all-done.1 = bf16[8,96,256]{2,1,0:T(8,128)(2,1)S(1)} async-done(((bf16[8,96,256]{2,1,0:T(8,128)(2,1)}), bf16[8,96,256]{2,1,0:T(8,128)(2,1)S(1)}, u32[]{:S(2)}, u32[]{:S(2)}) %all-to-all-start.1) | async-done | bytes 393248 | tf_op jit(solution)/shard_map/all_to_all | solution.py:84
  25.1 3.6 %all-to-all-start = ((bf16[8,96,512]{2,1,0:T(8,128)(2,1)}), bf16[8,96,512]{2,1,0:T(8,128)(2,1)S(1)}, u32[]{:S(2)}, u32[]{:S(2)}) async-start(bf16[8,96,512]{2,1,0:T(8,128)(2,1)} %bitcast.61), calls=%async_computation | async-start | bytes 1572864 | tf_op jit(solution)/shard_map/all_to_all | solution.py:84
  28.8 1.5 %collective-permute-start.3 = (bf16[768,256]{1,0:T(8,128)(2,1)S(1)}, bf16[768,256]{1,0:T(8,128)(2,1)}, u32[]{:S(2)}, u32[]{:S(2)}) collective-permute-start(bf16[768,256]{1,0:T(8,128)(2,1)S(1)} %bitcast.58), channel_id=1, source_target_pairs={{0,2},{1,3},{2,0},{3,1},{4,6},{5,7},{6,4},{7,5},{8,10},{9,11},{10,... | collective-permute-start | bytes 1179656 | tf_op jit(solution)/shard_map/ppermute | solution.py:87
  30.3 18.6 %all-to-all-done = bf16[8,96,512]{2,1,0:T(8,128)(2,1)S(1)} async-done(((bf16[8,96,512]{2,1,0:T(8,128)(2,1)}), bf16[8,96,512]{2,1,0:T(8,128)(2,1)S(1)}, u32[]{:S(2)}, u32[]{:S(2)}) %all-to-all-start) | async-done | bytes 786464 | tf_op jit(solution)/shard_map/all_to_all | solution.py:84
  48.9 1.5 %collective-permute-start = (bf16[768,512]{1,0:T(8,128)(2,1)S(1)}, bf16[768,512]{1,0:T(8,128)(2,1)}, u32[]{:S(2)}, u32[]{:S(2)}) collective-permute-start(bf16[768,512]{1,0:T(8,128)(2,1)S(1)} %bitcast.55), channel_id=1, source_target_pairs={{0,2},{1,3},{2,0},{3,1},{4,6},{5,7},{6,4},{7,5},{8,10},{9,11},{10,... | collective-permute-start | bytes 2359304 | tf_op jit(solution)/shard_map/ppermute | solution.py:87
  54.1 12.8 %collective-permute-done = bf16[768,512]{1,0:T(8,128)(2,1)} collective-permute-done((bf16[768,512]{1,0:T(8,128)(2,1)S(1)}, bf16[768,512]{1,0:T(8,128)(2,1)}, u32[]{:S(2)}, u32[]{:S(2)}) %collective-permute-start) | collective-permute-done | bytes 786464 | tf_op jit(solution)/shard_map/ppermute | solution.py:87
  66.9 3.5 %multiply_convert_fusion.2 = (bf16[768,1024]{1,0:T(8,128)(2,1)}, f32[768,1024]{1,0:T(8,128)S(1)}) fusion(bf16[768,1024]{1,0:T(8,128)(2,1)S(1)} %constant_dynamic-update-slice_fusion.6, bf16[1,1024,1024]{2,1,0:T(8,128)(2,1)S(1)} %copy-done), kind=kOutput, calls=%fused_computation.14 | convolution fusion | flops 1617690624 | bytes 8388608 | tf_op jit(solution)/shard_map/dot_general | solution.py:116
  72.8 5.0 %fusion.9 = bf16[768,1024]{1,0:T(8,128)(2,1)S(1)} fusion(f32[768,1024]{1,0:T(8,128)S(1)} %get-tuple-element.20, bf16[768,2048]{1,0:T(8,128)(2,1)S(1)} %constant_dynamic-update-slice_fusion.10, bf16[1,1024,2048]{2,1,0:T(8,128)(2,1)S(1)} %copy-done.5), kind=kOutput, calls=%fused_computation.13 | convolution fusion | flops 3236954112 | bytes 12058624 | tf_op jit(solution)/shard_map/dot_general | solution.py:119
  77.8 1.8 %fusion.12 = f32[768,1024]{1,0:T(8,128)S(1)} fusion(bf16[768,1024]{1,0:T(8,128)(2,1)S(1)} %fusion.9, bf16[1,1024,1024]{2,1,0:T(8,128)(2,1)S(1)} %copy-done), kind=kOutput, calls=%fused_computation.15 | convolution fusion | flops 1610612736 | bytes 6815744 | tf_op jit(solution)/shard_map/dot_general | solution.py:123
  82.9 3.4 %collective-permute-done.6 = f32[512,768]{0,1:T(8,128)} collective-permute-done((f32[512,768]{0,1:T(8,128)}, f32[512,768]{0,1:T(8,128)}, u32[]{:S(2)}, u32[]{:S(2)}) %collective-permute-start.6) | collective-permute-done | bytes 1572896 | tf_op jit(solution)/shard_map/ppermute | solution.py:50
  86.3 1.9 %maximum_add_fusion = f32[512,768]{0,1:T(8,128)S(1)} fusion(f32[512,768]{0,1:T(8,128)} %collective-permute-done.6, f32[256,768]{0,1:T(8,128)} %get-tuple-element.6, f32[256,768]{0,1:T(8,128)S(1)} %get-tuple-element.3), kind=kLoop, calls=%fused_computation.20 | loop fusion | flops 786432 | bytes 4718592 | tf_op jit(solution)/shard_map/add | solution.py:50
  88.3 1.6 %collective-permute-start.7 = (bf16[256,768]{0,1:T(8,128)(2,1)S(1)}, bf16[256,768]{0,1:T(8,128)(2,1)S(1)}, u32[]{:S(2)}, u32[]{:S(2)}) collective-permute-start(bf16[256,768]{0,1:T(8,128)(2,1)S(1)} %slice.46), channel_id=1, source_target_pairs={{0,2},{1,3},{2,0},{3,1},{4,6},{5,7},{6,4},{7,5},{8,10},{9,11},{10,... | collective-permute-start | bytes 1179656 | tf_op jit(solution)/shard_map/ppermute | solution.py:52
  89.9 5.0 %fusion.2 = bf16[1,1024,2048]{2,1,0:T(8,128)(2,1)} fusion(bf16[768,1024]{1,0:T(8,128)(2,1)S(1)} %copy-done.8, bf16[768,2048]{1,0:T(8,128)(2,1)S(1)} %copy-done.2), kind=kOutput, calls=%fused_computation.6 | convolution fusion | flops 3225419776 | bytes 8912896 | tf_op jit(solution)/shard_map/dot_general | solution.py:142
  94.9 4.8 %collective-permute-done.7 = bf16[256,768]{0,1:T(8,128)(2,1)S(1)} collective-permute-done((bf16[256,768]{0,1:T(8,128)(2,1)S(1)}, bf16[256,768]{0,1:T(8,128)(2,1)S(1)}, u32[]{:S(2)}, u32[]{:S(2)}) %collective-permute-start.7) | collective-permute-done | bytes 393248 | tf_op jit(solution)/shard_map/ppermute | solution.py:52
  100.0 2.1 %collective-permute-start.8 = (bf16[256,96]{0,1:T(8,128)(2,1)S(1)}, bf16[256,96]{0,1:T(8,128)(2,1)S(1)}, u32[]{:S(2)}, u32[]{:S(2)}) collective-permute-start(bf16[256,96]{0,1:T(8,128)(2,1)S(1)} %get-tuple-element.13), channel_id=1, source_target_pairs={{0,4},{4,0},{8,12},{12,8},{16,20},{20,16},{24,28},{28,24},{1,5},{5... | collective-permute-start | bytes 147464 | tf_op jit(solution)/shard_map/ppermute | solution.py:21
  102.1 3.2 %fusion.16 = bf16[1,1024,1024]{2,1,0:T(8,128)(2,1)} fusion(bf16[768,1024]{1,0:T(8,128)(2,1)S(1)} %copy-done.4, bf16[768,1024]{1,0:T(8,128)(2,1)S(1)} %copy-done.7), kind=kOutput, calls=%fused_computation.19 | convolution fusion | flops 1612709888 | bytes 5242880 | tf_op jit(solution)/shard_map/dot_general | solution.py:139
  105.3 1.8 %collective-permute-start.14 = (bf16[256,96]{0,1:T(8,128)(2,1)S(1)}, bf16[256,96]{0,1:T(8,128)(2,1)S(1)}, u32[]{:S(2)}, u32[]{:S(2)}) collective-permute-start(bf16[256,96]{0,1:T(8,128)(2,1)S(1)} %get-tuple-element.7), channel_id=1, source_target_pairs={{0,28},{4,24},{8,20},{12,16},{16,12},{20,8},{24,4},{28,0},{1,29},{... | collective-permute-start | bytes 147464 | tf_op jit(solution)/shard_map/ppermute | solution.py:21
  107.1 1.5 %collective-permute-start.13 = (bf16[256,96]{0,1:T(8,128)(2,1)S(1)}, bf16[256,96]{0,1:T(8,128)(2,1)S(1)}, u32[]{:S(2)}, u32[]{:S(2)}) collective-permute-start(bf16[256,96]{0,1:T(8,128)(2,1)S(1)} %get-tuple-element.8), channel_id=1, source_target_pairs={{0,24},{4,28},{8,16},{12,20},{16,8},{20,12},{24,0},{28,4},{1,25},{... | collective-permute-start | bytes 147464 | tf_op jit(solution)/shard_map/ppermute | solution.py:21
  108.6 4.4 %collective-permute-start.11 = (bf16[256,96]{0,1:T(8,128)(2,1)S(1)}, bf16[256,96]{0,1:T(8,128)(2,1)S(1)}, u32[]{:S(2)}, u32[]{:S(2)}) collective-permute-start(bf16[256,96]{0,1:T(8,128)(2,1)S(1)} %get-tuple-element.10), channel_id=1, source_target_pairs={{0,16},{4,20},{8,24},{12,28},{16,0},{20,4},{24,8},{28,12},{1,17},{... | collective-permute-start | bytes 147464 | tf_op jit(solution)/shard_map/ppermute | solution.py:21
  113.0 4.1 %collective-permute-done.9 = bf16[256,96]{0,1:T(8,128)(2,1)S(1)} collective-permute-done((bf16[256,96]{0,1:T(8,128)(2,1)S(1)}, bf16[256,96]{0,1:T(8,128)(2,1)S(1)}, u32[]{:S(2)}, u32[]{:S(2)}) %collective-permute-start.9) | collective-permute-done | bytes 49184 | tf_op jit(solution)/shard_map/ppermute | solution.py:21
  117.1 5.0 %collective-permute-done.10 = bf16[256,96]{0,1:T(8,128)(2,1)S(1)} collective-permute-done((bf16[256,96]{0,1:T(8,128)(2,1)S(1)}, bf16[256,96]{0,1:T(8,128)(2,1)S(1)}, u32[]{:S(2)}, u32[]{:S(2)}) %collective-permute-start.10) | collective-permute-done | bytes 49184 | tf_op jit(solution)/shard_map/ppermute | solution.py:21
  (74 shorter events, 14.9 us)
Async XLA Ops:
  0.6 66.2 %copy-start = (bf16[1,1024,1024]{2,1,0:T(8,128)(2,1)S(1)}, bf16[1,1024,1024]{2,1,0:T(8,128)(2,1)}, u32[]{:S(2)}) copy-start(bf16[1,1024,1024]{2,1,0:T(8,128)(2,1)} %param.10) | copy-start | bytes 6291460
  6.2 19.0 %all-to-all-start.1 = ((bf16[8,96,256]{2,1,0:T(8,128)(2,1)}), bf16[8,96,256]{2,1,0:T(8,128)(2,1)S(1)}, u32[]{:S(2)}, u32[]{:S(2)}) async-start(bf16[8,96,256]{2,1,0:T(8,128)(2,1)} %bitcast.13), calls=%async_computation.1 | async-start | bytes 786432 | tf_op jit(solution)/shard_map/all_to_all | solution.py:84
  25.1 23.8 %all-to-all-start = ((bf16[8,96,512]{2,1,0:T(8,128)(2,1)}), bf16[8,96,512]{2,1,0:T(8,128)(2,1)S(1)}, u32[]{:S(2)}, u32[]{:S(2)}) async-start(bf16[8,96,512]{2,1,0:T(8,128)(2,1)} %bitcast.61), calls=%async_computation | async-start | bytes 1572864 | tf_op jit(solution)/shard_map/all_to_all | solution.py:84
  28.8 21.7 %collective-permute-start.3 = (bf16[768,256]{1,0:T(8,128)(2,1)S(1)}, bf16[768,256]{1,0:T(8,128)(2,1)}, u32[]{:S(2)}, u32[]{:S(2)}) collective-permute-start(bf16[768,256]{1,0:T(8,128)(2,1)S(1)} %bitcast.58), channel_id=1, source_target_pairs={{0,2},{1,3},{2,0},{3,1},{4,6},{5,7},{6,4},{7,5},{8,10},{9,11},{10,... | collective-permute-start | bytes 1179656 | tf_op jit(solution)/shard_map/ppermute | solution.py:87
  48.9 18.0 %collective-permute-start = (bf16[768,512]{1,0:T(8,128)(2,1)S(1)}, bf16[768,512]{1,0:T(8,128)(2,1)}, u32[]{:S(2)}, u32[]{:S(2)}) collective-permute-start(bf16[768,512]{1,0:T(8,128)(2,1)S(1)} %bitcast.55), channel_id=1, source_target_pairs={{0,2},{1,3},{2,0},{3,1},{4,6},{5,7},{6,4},{7,5},{8,10},{9,11},{10,... | collective-permute-start | bytes 2359304 | tf_op jit(solution)/shard_map/ppermute | solution.py:87
  50.4 1.9 %collective-permute-start.4 = (bf16[768,256]{1,0:T(8,128)(2,1)S(1)}, bf16[768,256]{1,0:T(8,128)(2,1)}, u32[]{:S(2)}, u32[]{:S(2)}) collective-permute-start(bf16[768,256]{1,0:T(8,128)(2,1)S(1)} %bitcast.59), channel_id=1, source_target_pairs={{0,1},{1,0},{2,3},{3,2},{4,5},{5,4},{6,7},{7,6},{8,9},{9,8},{10,11... | collective-permute-start | bytes 1179656 | tf_op jit(solution)/shard_map/ppermute | solution.py:91
  50.4 3.6 %collective-permute-start.5 = (bf16[768,256]{1,0:T(8,128)(2,1)}, bf16[768,256]{1,0:T(8,128)(2,1)S(1)}, u32[]{:S(2)}, u32[]{:S(2)}) collective-permute-start(bf16[768,256]{1,0:T(8,128)(2,1)} %collective-permute-done.3), channel_id=1, source_target_pairs={{0,1},{1,0},{2,3},{3,2},{4,5},{5,4},{6,7},{7,6},{8,9},{9,8},{10,11... | collective-permute-start | bytes 1179656 | tf_op jit(solution)/shard_map/ppermute | solution.py:91
  53.3 18.5 %collective-permute-start.1 = (bf16[768,512]{1,0:T(8,128)(2,1)S(1)}, bf16[768,512]{1,0:T(8,128)(2,1)S(1)}, u32[]{:S(2)}, u32[]{:S(2)}) collective-permute-start(bf16[768,512]{1,0:T(8,128)(2,1)S(1)} %bitcast.56), channel_id=1, source_target_pairs={{0,1},{1,0},{2,3},{3,2},{4,5},{5,4},{6,7},{7,6},{8,9},{9,8},{10,11... | collective-permute-start | bytes 2359304 | tf_op jit(solution)/shard_map/ppermute | solution.py:91
  54.1 16.3 %copy-start.3 = (bf16[768,1024]{1,0:T(8,128)(2,1)}, bf16[768,1024]{1,0:T(8,128)(2,1)S(1)}, u32[]{:S(2)}) copy-start(bf16[768,1024]{1,0:T(8,128)(2,1)S(1)} %constant_dynamic-update-slice_fusion.6) | copy-start | bytes 4718596
  66.9 5.0 %collective-permute-start.2 = (bf16[768,512]{1,0:T(8,128)(2,1)}, bf16[768,512]{1,0:T(8,128)(2,1)S(1)}, u32[]{:S(2)}, u32[]{:S(2)}) collective-permute-start(bf16[768,512]{1,0:T(8,128)(2,1)} %collective-permute-done), channel_id=1, source_target_pairs={{0,1},{1,0},{2,3},{3,2},{4,5},{5,4},{6,7},{7,6},{8,9},{9,8},{10,11... | collective-permute-start | bytes 2359304 | tf_op jit(solution)/shard_map/ppermute | solution.py:91
  72.0 5.8 %copy-start.1 = (bf16[768,2048]{1,0:T(8,128)(2,1)}, bf16[768,2048]{1,0:T(8,128)(2,1)S(1)}, u32[]{:S(2)}) copy-start(bf16[768,2048]{1,0:T(8,128)(2,1)S(1)} %constant_dynamic-update-slice_fusion.10) | copy-start | bytes 9437188
  82.4 3.9 %collective-permute-start.6 = (f32[512,768]{0,1:T(8,128)}, f32[512,768]{0,1:T(8,128)}, u32[]{:S(2)}, u32[]{:S(2)}) collective-permute-start(f32[512,768]{0,1:T(8,128)} %pad_maximum_fusion), channel_id=1, source_target_pairs={{0,1},{1,0},{2,3},{3,2},{4,5},{5,4},{6,7},{7,6},{8,9},{9,8},{10,11... | collective-permute-start | bytes 4718600 | tf_op jit(solution)/shard_map/ppermute | solution.py:50
  82.9 7.0 %copy-start.2 = (bf16[768,2048]{1,0:T(8,128)(2,1)S(1)}, bf16[768,2048]{1,0:T(8,128)(2,1)}, u32[]{:S(2)}) copy-start(bf16[768,2048]{1,0:T(8,128)(2,1)} %copy-done.1) | copy-start | bytes 9437188
  82.9 7.0 %copy-start.8 = (bf16[768,1024]{1,0:T(8,128)(2,1)S(1)}, bf16[768,1024]{1,0:T(8,128)(2,1)}, u32[]{:S(2)}) copy-start(bf16[768,1024]{1,0:T(8,128)(2,1)} %get-tuple-element.19) | copy-start | bytes 4718596
  88.3 13.8 %copy-start.4 = (bf16[768,1024]{1,0:T(8,128)(2,1)S(1)}, bf16[768,1024]{1,0:T(8,128)(2,1)}, u32[]{:S(2)}) copy-start(bf16[768,1024]{1,0:T(8,128)(2,1)} %copy-done.3) | copy-start | bytes 4718596
  88.3 13.8 %copy-start.7 = (bf16[768,1024]{1,0:T(8,128)(2,1)S(1)}, bf16[768,1024]{1,0:T(8,128)(2,1)}, u32[]{:S(2)}) copy-start(bf16[768,1024]{1,0:T(8,128)(2,1)} %copy-done.6) | copy-start | bytes 4718596
  88.3 11.5 %collective-permute-start.7 = (bf16[256,768]{0,1:T(8,128)(2,1)S(1)}, bf16[256,768]{0,1:T(8,128)(2,1)S(1)}, u32[]{:S(2)}, u32[]{:S(2)}) collective-permute-start(bf16[256,768]{0,1:T(8,128)(2,1)S(1)} %slice.46), channel_id=1, source_target_pairs={{0,2},{1,3},{2,0},{3,1},{4,6},{5,7},{6,4},{7,5},{8,10},{9,11},{10,... | collective-permute-start | bytes 1179656 | tf_op jit(solution)/shard_map/ppermute | solution.py:52
  100.0 12.9 %collective-permute-start.8 = (bf16[256,96]{0,1:T(8,128)(2,1)S(1)}, bf16[256,96]{0,1:T(8,128)(2,1)S(1)}, u32[]{:S(2)}, u32[]{:S(2)}) collective-permute-start(bf16[256,96]{0,1:T(8,128)(2,1)S(1)} %get-tuple-element.13), channel_id=1, source_target_pairs={{0,4},{4,0},{8,12},{12,8},{16,20},{20,16},{24,28},{28,24},{1,5},{5... | collective-permute-start | bytes 147464 | tf_op jit(solution)/shard_map/ppermute | solution.py:21
  105.3 16.8 %collective-permute-start.14 = (bf16[256,96]{0,1:T(8,128)(2,1)S(1)}, bf16[256,96]{0,1:T(8,128)(2,1)S(1)}, u32[]{:S(2)}, u32[]{:S(2)}) collective-permute-start(bf16[256,96]{0,1:T(8,128)(2,1)S(1)} %get-tuple-element.7), channel_id=1, source_target_pairs={{0,28},{4,24},{8,20},{12,16},{16,12},{20,8},{24,4},{28,0},{1,29},{... | collective-permute-start | bytes 147464 | tf_op jit(solution)/shard_map/ppermute | solution.py:21
  107.1 15.0 %collective-permute-start.13 = (bf16[256,96]{0,1:T(8,128)(2,1)S(1)}, bf16[256,96]{0,1:T(8,128)(2,1)S(1)}, u32[]{:S(2)}, u32[]{:S(2)}) collective-permute-start(bf16[256,96]{0,1:T(8,128)(2,1)S(1)} %get-tuple-element.8), channel_id=1, source_target_pairs={{0,24},{4,28},{8,16},{12,20},{16,8},{20,12},{24,0},{28,4},{1,25},{... | collective-permute-start | bytes 147464 | tf_op jit(solution)/shard_map/ppermute | solution.py:21
  108.6 13.5 %collective-permute-start.12 = (bf16[256,96]{0,1:T(8,128)(2,1)S(1)}, bf16[256,96]{0,1:T(8,128)(2,1)S(1)}, u32[]{:S(2)}, u32[]{:S(2)}) collective-permute-start(bf16[256,96]{0,1:T(8,128)(2,1)S(1)} %get-tuple-element.9), channel_id=1, source_target_pairs={{0,20},{4,16},{8,28},{12,24},{16,4},{20,0},{24,12},{28,8},{1,21},{... | collective-permute-start | bytes 147464 | tf_op jit(solution)/shard_map/ppermute | solution.py:21
  108.6 13.4 %collective-permute-start.11 = (bf16[256,96]{0,1:T(8,128)(2,1)S(1)}, bf16[256,96]{0,1:T(8,128)(2,1)S(1)}, u32[]{:S(2)}, u32[]{:S(2)}) collective-permute-start(bf16[256,96]{0,1:T(8,128)(2,1)S(1)} %get-tuple-element.10), channel_id=1, source_target_pairs={{0,16},{4,20},{8,24},{12,28},{16,0},{20,4},{24,8},{28,12},{1,17},{... | collective-permute-start | bytes 147464 | tf_op jit(solution)/shard_map/ppermute | solution.py:21
  112.9 4.1 %collective-permute-start.9 = (bf16[256,96]{0,1:T(8,128)(2,1)S(1)}, bf16[256,96]{0,1:T(8,128)(2,1)S(1)}, u32[]{:S(2)}, u32[]{:S(2)}) collective-permute-start(bf16[256,96]{0,1:T(8,128)(2,1)S(1)} %get-tuple-element.12), channel_id=1, source_target_pairs={{0,8},{4,12},{8,0},{12,4},{16,24},{20,28},{24,16},{28,20},{1,9},{5... | collective-permute-start | bytes 147464 | tf_op jit(solution)/shard_map/ppermute | solution.py:21
  117.0 5.0 %collective-permute-start.10 = (bf16[256,96]{0,1:T(8,128)(2,1)S(1)}, bf16[256,96]{0,1:T(8,128)(2,1)S(1)}, u32[]{:S(2)}, u32[]{:S(2)}) collective-permute-start(bf16[256,96]{0,1:T(8,128)(2,1)S(1)} %get-tuple-element.11), channel_id=1, source_target_pairs={{0,12},{4,8},{8,4},{12,0},{16,28},{20,24},{24,20},{28,16},{1,13},{... | collective-permute-start | bytes 147464 | tf_op jit(solution)/shard_map/ppermute | solution.py:21
  (2 other events, 4.3 us)
